TPU v7x, 32 devices: a whole 2x2x4 slice. The times are simulated.
32 devices in a mesh: group: 2 (over y), seq: 4 (over z), batch: 2 (over x), mp: 2 (over core).
Axes of the slice: x: 2, y: 2, z: 4, core: 2. Of those that a mesh axis runs over, the one named last changes fastest.
Arguments:
- features: bfloat16 [4, 512, 384], P(('group', 'batch'), 'seq'), parts along dimension 0, may hold values from -6 to 6
- noise: float32 [4, 512, 384], P(('group', 'batch'), 'seq'), parts along dimension 0, may hold values from -3 to 3
- conv_weight: bfloat16 [5, 384, 768], P(None, 'seq', 'mp'), may hold values from -0.125 to 0.125
- conv_bias: float32 [768], P('mp'), may hold values from -3 to 3
- norm_gain: float32 [768], replicated, may hold values from 0.25 to 1.75
- qkv_weight: bfloat16 [3, 768, 768], P(None, 'seq', 'mp'), may hold values from -1.010363 to 1.010363
- out_weight: bfloat16 [768, 768], P('mp', 'seq'), may hold values from -0.21875 to 0.21875
Outputs:
- block_out: bfloat16 [4, 256, 768], P(('group', 'batch'), 'seq', 'mp'), parts along dimension 0
- new_noise: float32 [4, 512, 384], P(('group', 'batch'), 'seq'), parts along dimension 0
There are 2 independent parts, one for each index of `group`. A program takes and returns all parts, laid end to end along the dimension named above; an argument that names none is the same for every part. Nothing has to cross between parts.
All inputs are finite; a program needn't handle non-finite values.
Results may differ from a plain program's by a relative error of at most 0.014.
Values may be sent and summed in bfloat16 or wider, within the bound.
No kernel may reach another device: no remote copies, remote signals or barrier semaphores. Data moves between devices by JAX's collectives and lax.ppermute only.
A program may use at most 64 MiB of HBM per device.

v0:
```python
import jax
import jax.numpy as jnp
from jax import lax
from jax.sharding import PartitionSpec as P

F = 768
HD = 96
KW = 5
step_size = 0.5
epsilon = 1e-06


def with_halo(cells, sides, width):
    for axis, dim in sides:
        count = lax.axis_size(axis)
        ends = count - 1
        head = lax.slice_in_dim(cells, 0, width, axis=dim)
        tail = lax.slice_in_dim(cells, cells.shape[dim] - width, cells.shape[dim], axis=dim)
        cells = jnp.concatenate(
            [
                lax.ppermute(tail, axis, [(i, (i + 1) % count) for i in range(ends)]),
                cells,
                lax.ppermute(head, axis, [((i + 1) % count, i) for i in range(ends)]),
            ],
            axis=dim,
        )
    return cells


def attend_rows(query, keys, values):
    key_total = keys.shape[0]
    block_len = min(512, key_total)
    head_size = keys.shape[1]
    score_scale = head_size ** (-0.5)
    key_blocks = keys.reshape(key_total // block_len, block_len, head_size)
    value_blocks = values.reshape(key_total // block_len, block_len, head_size)
    query_count = query.shape[0]

    def find_top(carry, key_block):
        row_top, row_mass = carry
        scores = jnp.dot(query, key_block.T, preferred_element_type=jnp.float32) * score_scale
        new_top = jnp.maximum(row_top, jnp.max(scores, axis=1))
        row_mass = row_mass * jnp.exp(row_top - new_top) + jnp.sum(
            jnp.exp(scores - new_top[:, None]), axis=1
        )
        return ((new_top, row_mass), None)

    start_top = jnp.full((query_count,), -1e30, jnp.float32)
    (row_top, row_mass), _ = lax.scan(
        find_top, (start_top, jnp.zeros((query_count,), jnp.float32)), key_blocks
    )
    log_mass = row_top + jnp.log(row_mass)

    def collect(running, blocks):
        key_block, value_block = blocks
        scores = jnp.dot(query, key_block.T, preferred_element_type=jnp.float32) * score_scale
        soft_weights = jnp.exp(scores - log_mass[:, None]).astype(jnp.bfloat16)
        return (
            running + jnp.dot(soft_weights, value_block, preferred_element_type=jnp.float32),
            None,
        )

    running, _ = lax.scan(
        collect, jnp.zeros((query_count, head_size), jnp.float32), (key_blocks, value_blocks)
    )
    return (running.astype(jnp.bfloat16), log_mass)


def attend_back(query, keys, values, attended, log_mass, out_grad):
    key_total = keys.shape[0]
    block_len = min(512, key_total)
    head_size = keys.shape[1]
    score_scale = head_size ** (-0.5)
    key_blocks = keys.reshape(key_total // block_len, block_len, head_size)
    value_blocks = values.reshape(key_total // block_len, block_len, head_size)
    row_dot = jnp.sum(out_grad.astype(jnp.float32) * attended.astype(jnp.float32), axis=1)

    def step_back(query_acc, blocks):
        key_block, value_block = blocks
        scores = jnp.dot(query, key_block.T, preferred_element_type=jnp.float32) * score_scale
        exp_weights = jnp.exp(scores - log_mass[:, None])
        value_part = jnp.einsum(
            "qk,qd->kd",
            exp_weights.astype(jnp.bfloat16),
            out_grad,
            preferred_element_type=jnp.float32,
        )
        prob_grad = jnp.dot(out_grad, value_block.T, preferred_element_type=jnp.float32)
        score_grad = (exp_weights * (prob_grad - row_dot[:, None])).astype(jnp.bfloat16)
        query_acc = (
            query_acc
            + jnp.dot(score_grad, key_block, preferred_element_type=jnp.float32) * score_scale
        )
        key_part = (
            jnp.einsum("qk,qd->kd", score_grad, query, preferred_element_type=jnp.float32)
            * score_scale
        )
        return (query_acc, jnp.concatenate([key_part, value_part], axis=1))

    query_grad, keyval_parts = lax.scan(
        step_back, jnp.zeros((query.shape[0], head_size), jnp.float32), (key_blocks, value_blocks)
    )
    return (query_grad, keyval_parts.reshape(key_total, 2 * head_size))


def forward(stack, conv_weight, conv_bias, norm_gain, qkv_weight, out_weight):
    pass_count, positions, channels = stack.shape
    reach = KW // 2
    half_width = conv_weight.shape[2]
    padded_input = with_halo(stack, (("seq", 1),), reach)
    running = jnp.zeros((pass_count, positions, half_width), jnp.float32)
    piece = lax.all_gather(conv_weight, "seq", axis=1, tiled=True)
    for offset in range(piece.shape[0]):
        running = running + jnp.einsum(
            "ptc,cf->ptf",
            padded_input[:, offset : offset + positions],
            piece[offset],
            preferred_element_type=jnp.float32,
        )
    pre_act = running + conv_bias
    paired = jax.nn.gelu(pre_act).reshape(pass_count, positions // 2, 2, half_width)
    pooled = (0.5 * (paired[:, :, 0] + paired[:, :, 1])).astype(jnp.bfloat16)
    pooled_wide = lax.optimization_barrier(pooled).astype(jnp.float32)
    whole = lax.all_gather(pooled, "mp", axis=2, tiled=True)
    whole_wide = whole.astype(jnp.float32)
    row_scale = lax.rsqrt(jnp.mean(whole_wide * whole_wide, axis=2, keepdims=True) + epsilon)
    normed = (whole_wide * row_scale * norm_gain).astype(jnp.bfloat16)
    rows = positions // 2
    proj_width = qkv_weight.shape[2]
    projected = jnp.einsum(
        "prf,jfh->jprh",
        normed,
        lax.all_gather(qkv_weight, "seq", axis=1, tiled=True),
        preferred_element_type=jnp.float32,
    ).astype(jnp.bfloat16)
    head_size = HD
    head_count = proj_width // head_size
    devices = lax.axis_size("seq")
    query_groups = devices // head_count
    sub_rows = rows // query_groups
    query_send = (
        projected[0]
        .reshape(pass_count, query_groups, sub_rows, head_count, head_size)
        .transpose(3, 1, 0, 2, 4)
        .reshape(devices, pass_count, sub_rows * head_size)
    )
    keyval = jnp.concatenate(
        [
            projected[1].reshape(pass_count, rows, head_count, head_size),
            projected[2].reshape(pass_count, rows, head_count, head_size),
        ],
        axis=3,
    )
    keyval_flat = keyval.transpose(2, 0, 1, 3).reshape(
        head_count, 1, pass_count, rows * 2 * head_size
    )
    keyval_send = jnp.broadcast_to(
        keyval_flat, (head_count, query_groups, pass_count, rows * 2 * head_size)
    ).reshape(devices, pass_count, rows * 2 * head_size)
    query_in, keyval_in = (
        lax.all_to_all(query_send, "seq", split_axis=0, concat_axis=2, tiled=True),
        lax.all_to_all(keyval_send, "seq", split_axis=0, concat_axis=2, tiled=True),
    )
    query_heads = query_in.reshape(pass_count, devices * sub_rows, head_size)
    keyval_heads = keyval_in.reshape(pass_count, devices * rows, 2 * head_size)
    outputs = []
    masses = []
    for index in range(pass_count):
        out_now, mass_now = attend_rows(
            query_heads[index],
            keyval_heads[index, :, :head_size],
            keyval_heads[index, :, head_size:],
        )
        outputs.append(out_now)
        masses.append(mass_now)
    attended_heads = jnp.stack(outputs)
    log_mass = jnp.stack(masses)
    out_send = attended_heads.reshape(pass_count, devices, sub_rows * head_size).transpose(1, 0, 2)
    out_back = lax.all_to_all(out_send, "seq", split_axis=0, concat_axis=0, tiled=True)
    attended = (
        out_back.reshape(head_count, query_groups, pass_count, sub_rows, head_size)
        .transpose(2, 1, 3, 0, 4)
        .reshape(pass_count, rows, proj_width)
    )
    terms = jnp.einsum(
        "prh,hf->prf",
        attended,
        lax.all_gather(out_weight, "seq", axis=1, tiled=True),
        preferred_element_type=jnp.float32,
    )
    mixed = (
        lax.psum_scatter(terms.astype(jnp.bfloat16), "mp", scatter_dimension=2, tiled=True).astype(
            jnp.float32
        )
        + pooled_wide
    )
    return (
        pre_act,
        pooled_wide,
        whole_wide,
        row_scale,
        query_heads,
        keyval_heads,
        attended_heads,
        log_mass,
        mixed,
    )


def shards(features, noise, conv_weight, conv_bias, norm_gain, qkv_weight, out_weight):
    clean = features[0]
    moved = (clean.astype(jnp.float32) + noise[0]).astype(jnp.bfloat16)
    joint = forward(
        jnp.stack([clean, moved]), conv_weight, conv_bias, norm_gain, qkv_weight, out_weight
    )
    clean_run = [item[0:1] for item in joint]
    moved_run = [item[1:2] for item in joint]
    (
        pre_act,
        pooled_wide,
        whole_wide,
        row_scale,
        query_heads,
        keyval_heads,
        attended_heads,
        log_mass,
        mixed,
    ) = [item[0] for item in moved_run]
    clean_mixed = clean_run[8][0]
    rows, half_width = pooled_wide.shape
    positions = pre_act.shape[0]
    proj_width = qkv_weight.shape[2]
    head_size = HD
    head_count = proj_width // head_size
    devices = lax.axis_size("seq")
    query_groups = devices // head_count
    sub_rows = rows // query_groups
    difference = mixed - clean_mixed
    difference_half = difference.astype(jnp.bfloat16)
    difference_whole = lax.all_gather(difference_half, "mp", axis=1, tiled=True)
    out_grad = jnp.einsum(
        "rf,hf->rh",
        difference_whole,
        lax.all_gather(out_weight, "seq", axis=1, tiled=True),
        preferred_element_type=jnp.float32,
    ).astype(jnp.bfloat16)
    grad_send = (
        out_grad.reshape(query_groups, sub_rows, head_count, head_size)
        .transpose(2, 0, 1, 3)
        .reshape(devices, sub_rows * head_size)
    )
    grad_in = lax.all_to_all(grad_send, "seq", split_axis=0, concat_axis=1, tiled=True)
    grad_heads = grad_in.reshape(devices * sub_rows, head_size)
    query_grad, keyval_grad = attend_back(
        query_heads,
        keyval_heads[:, :head_size],
        keyval_heads[:, head_size:],
        attended_heads,
        log_mass,
        grad_heads,
    )
    query_back, keyval_back = (
        lax.all_to_all(
            query_grad.reshape(devices, sub_rows * head_size).astype(jnp.bfloat16),
            "seq",
            split_axis=0,
            concat_axis=0,
            tiled=True,
        ).astype(jnp.float32),
        lax.all_to_all(
            keyval_grad.reshape(devices, rows * 2 * head_size).astype(jnp.bfloat16),
            "seq",
            split_axis=0,
            concat_axis=0,
            tiled=True,
        ).astype(jnp.float32),
    )
    query_rows = (
        query_back.reshape(head_count, query_groups, sub_rows, head_size)
        .transpose(1, 2, 0, 3)
        .reshape(rows, proj_width)
        .astype(jnp.bfloat16)
    )
    keyval_rows = jnp.sum(keyval_back.reshape(head_count, query_groups, rows, 2, head_size), axis=1)
    key_rows = (
        keyval_rows[:, :, 0].transpose(1, 0, 2).reshape(rows, proj_width).astype(jnp.bfloat16)
    )
    value_rows = (
        keyval_rows[:, :, 1].transpose(1, 0, 2).reshape(rows, proj_width).astype(jnp.bfloat16)
    )
    grads = jnp.stack([query_rows, key_rows, value_rows])
    normed_terms = jnp.einsum(
        "jrh,jfh->rf",
        grads,
        lax.all_gather(qkv_weight, "seq", axis=1, tiled=True),
        preferred_element_type=jnp.float32,
    )
    offset_mp = lax.axis_index("mp") * half_width
    gain_own = lax.dynamic_slice_in_dim(norm_gain, offset_mp, half_width, 0)
    normed_grad = lax.psum_scatter(
        normed_terms.astype(jnp.bfloat16), "mp", scatter_dimension=1, tiled=True
    ).astype(jnp.float32)
    weighted = lax.psum(jnp.sum(normed_grad * gain_own * pooled_wide, axis=1, keepdims=True), "mp")
    pooled_grad = (
        difference + row_scale * gain_own * normed_grad - pooled_wide * row_scale**3 * weighted / F
    )
    spread = jnp.broadcast_to((0.5 * pooled_grad)[:, None, :], (rows, 2, half_width)).reshape(
        positions, half_width
    )
    gelu_back = jax.vjp(jax.nn.gelu, pre_act)[1]
    pre_grad = gelu_back(spread)[0].astype(jnp.bfloat16)
    reach = KW // 2
    padded = with_halo(pre_grad, (("seq", 0),), reach)
    piece = lax.all_gather(conv_weight, "seq", axis=1, tiled=True)
    running = jnp.zeros((positions, piece.shape[1]), jnp.float32)
    for offset in range(piece.shape[0]):
        lower = 2 * reach - offset
        running = running + jnp.einsum(
            "tf,cf->tc",
            padded[lower : lower + positions],
            piece[offset],
            preferred_element_type=jnp.float32,
        )
    input_grad = lax.psum(running.astype(jnp.bfloat16), "mp").astype(jnp.float32)
    new_noise = noise[0] + step_size * input_grad * lax.rsqrt(
        jnp.mean(input_grad * input_grad, axis=1, keepdims=True) + epsilon
    )
    return (clean_mixed.astype(jnp.bfloat16)[None], new_noise[None])


def solution(mesh):
    return jax.shard_map(
        shards,
        mesh=mesh,
        in_specs=(
            P(("group", "batch"), "seq", None),
            P(("group", "batch"), "seq", None),
            P(None, "seq", "mp"),
            P("mp"),
            P(),
            P(None, "seq", "mp"),
            P("mp", "seq"),
        ),
        out_specs=(P(("group", "batch"), "seq", "mp"), P(("group", "batch"), "seq", None)),
        check_vma=False,
    )
```

profile of v0, /device:TPU:0, one launch (start us, length us, event | category | flops | bytes accessed | tf_op | source)
XLA Modules:
  0.0 244.7 jit_solution(5682853137255914638)
XLA Ops:
  10.4 4.9 %collective-permute-start = (bf16[2,2,384]{2,1,0:T(2,128)(2,1)S(1)}, bf16[2,2,384]{2,1,0:T(2,128)(2,1)S(1)}, u32[]{:S(2)}, u32[]{:S(2)}) collective-permute-start(bf16[2,2,384]{2,1,0:T(2,128)(2,1)S(1)} %get-tuple-element.88), channel_id=1, source_target_pairs={{0,4},{4,8},{8,12},{1,5},{5,9},{9,13},{2,6},{6,10},{10,14},{3,7},{... | collective-permute-start | bytes 9224 | tf_op jit(solution)/shard_map/ppermute | solution.py:21
  15.4 1.3 collective-permute-start.1
  16.7 4.2 %collective-permute-done.1 = bf16[2,2,384]{2,1,0:T(2,128)(2,1)S(1)} collective-permute-done((bf16[2,2,384]{2,1,0:T(2,128)(2,1)S(1)}, bf16[2,2,384]{2,1,0:T(2,128)(2,1)S(1)}, u32[]{:S(2)}, u32[]{:S(2)}) %collective-permute-start.1) | collective-permute-done | bytes 3104 | tf_op jit(solution)/shard_map/ppermute | solution.py:23
  20.9 26.7 %all-gather.4.cloned.1.call-done = bf16[5,384,384]{2,1,0:T(8,128)(2,1)} async-done(((bf16[5,96,384]{2,1,0:T(8,128)(2,1)}), bf16[5,384,384]{2,1,0:T(8,128)(2,1)}) %all-gather.4.cloned.1.call-update) | async-done | bytes 1474576 | tf_op jit(solution)/shard_map/all_gather | solution.py:112
  47.6 1.3 fusion.38
  51.9 1.9 all-gather
  54.0 34.5 %all-gather.6.cloned.1.call-done = bf16[3,768,384]{2,1,0:T(8,128)(2,1)} async-done(((bf16[3,192,384]{2,1,0:T(8,128)(2,1)}), bf16[3,768,384]{2,1,0:T(8,128)(2,1)}) %all-gather.6.cloned.1.call-update) | async-done | bytes 1769488 | tf_op jit(solution)/shard_map/all_gather | solution.py:133
  88.5 2.0 fusion.8
  91.5 3.3 %all-to-all-start = ((bf16[4,2,6144]{2,1,0:T(2,128)(2,1)}), bf16[4,2,6144]{2,1,0:T(2,128)(2,1)S(1)}, u32[]{:S(2)}, u32[]{:S(2)}) async-start(bf16[4,2,6144]{2,1,0:T(2,128)(2,1)} %reshape.242), calls=%async_computation | async-start | bytes 196608 | tf_op jit(solution)/shard_map/all_to_all | solution.py:161
  96.3 4.3 %all-to-all-done = bf16[4,2,6144]{2,1,0:T(2,128)(2,1)S(1)} async-done(((bf16[4,2,6144]{2,1,0:T(2,128)(2,1)}), bf16[4,2,6144]{2,1,0:T(2,128)(2,1)S(1)}, u32[]{:S(2)}, u32[]{:S(2)}) %all-to-all-start) | async-done | bytes 98336 | tf_op jit(solution)/shard_map/all_to_all | solution.py:161
  100.6 3.4 %all-to-all-start.1 = ((bf16[4,2,12288]{2,1,0:T(2,128)(2,1)}), bf16[4,2,12288]{2,1,0:T(2,128)(2,1)S(1)}, u32[]{:S(2)}, u32[]{:S(2)}) async-start(bf16[4,2,12288]{2,1,0:T(2,128)(2,1)} %reshape_reshape.4), calls=%async_computation.1 | async-start | bytes 393216 | tf_op jit(solution)/shard_map/all_to_all | solution.py:162
  104.6 5.5 %all-to-all-done.1 = bf16[4,2,12288]{2,1,0:T(2,128)(2,1)S(1)} async-done(((bf16[4,2,12288]{2,1,0:T(2,128)(2,1)}), bf16[4,2,12288]{2,1,0:T(2,128)(2,1)S(1)}, u32[]{:S(2)}, u32[]{:S(2)}) %all-to-all-start.1) | async-done | bytes 196640 | tf_op jit(solution)/shard_map/all_to_all | solution.py:162
  113.2 3.3 %all-to-all-start.2 = ((bf16[4,2,6144]{2,1,0:T(2,128)(2,1)}), bf16[4,2,6144]{2,1,0:T(2,128)(2,1)S(1)}, u32[]{:S(2)}, u32[]{:S(2)}) async-start(bf16[4,2,6144]{2,1,0:T(2,128)(2,1)} %copy.103), calls=%async_computation.2 | async-start | bytes 196608 | tf_op jit(solution)/shard_map/all_to_all | solution.py:179
  116.6 16.8 %all_gather.21 = bf16[384,768]{0,1:T(8,128)(2,1)S(1)} all-gather(bf16[384,192]{0,1:T(8,128)(2,1)S(1)} %copy-done.8), channel_id=1, replica_groups=mesh['group'=2,'seq'=4,'batch'=2,'mp'=2] {'seq'}, dimensions={1}, use_global_device_ids=true | all-gather | bytes 737280 | tf_op jit(solution)/shard_map/all_gather | solution.py:188
  137.8 5.3 %reduce-scatter.7.cloned.1.call-done = bf16[384,128]{1,0:T(8,128)(2,1)} async-done(((bf16[768,128]{1,0:T(8,128)(2,1)}), bf16[384,128]{1,0:T(8,128)(2,1)}) %reduce-scatter.7.cloned.1.call-update) | async-done | bytes 98320
  144.3 1.9 all_gather.22
  148.7 4.8 %all-to-all-start.3 = ((bf16[4,2,3072]{2,1,0:T(2,128)(2,1)}), bf16[4,2,3072]{2,1,0:T(2,128)(2,1)S(1)}, u32[]{:S(2)}, u32[]{:S(2)}) async-start(bf16[4,2,3072]{2,1,0:T(2,128)(2,1)} %reshape.271), calls=%async_computation.3 | async-start | bytes 98304 | tf_op jit(solution)/shard_map/all_to_all | solution.py:252
  153.7 5.5 %all-to-all-done.3 = bf16[4,2,3072]{2,1,0:T(2,128)(2,1)S(1)} async-done(((bf16[4,2,3072]{2,1,0:T(2,128)(2,1)}), bf16[4,2,3072]{2,1,0:T(2,128)(2,1)S(1)}, u32[]{:S(2)}, u32[]{:S(2)}) %all-to-all-start.3) | async-done | bytes 49184 | tf_op jit(solution)/shard_map/all_to_all | solution.py:252
  162.6 3.5 %all-to-all-start.4 = ((bf16[4,2,3072]{2,1,0:T(2,128)(2,1)}), bf16[4,2,3072]{2,1,0:T(2,128)(2,1)S(1)}, u32[]{:S(2)}, u32[]{:S(2)}) async-start(bf16[4,2,3072]{2,1,0:T(2,128)(2,1)} %reshape.275), calls=%async_computation.4 | async-start | bytes 98304 | tf_op jit(solution)/shard_map/all_to_all | solution.py:263
  166.3 1.2 reduce.10
  168.3 3.2 %all-to-all-done.4 = bf16[4,2,3072]{2,1,0:T(2,128)(2,1)S(1)} async-done(((bf16[4,2,3072]{2,1,0:T(2,128)(2,1)}), bf16[4,2,3072]{2,1,0:T(2,128)(2,1)S(1)}, u32[]{:S(2)}, u32[]{:S(2)}) %all-to-all-start.4) | async-done | bytes 49184 | tf_op jit(solution)/shard_map/all_to_all | solution.py:263
  172.1 3.9 %all-to-all-start.5 = ((bf16[4,2,6144]{2,1,0:T(2,128)(2,1)}), bf16[4,2,6144]{2,1,0:T(2,128)(2,1)}, u32[]{:S(2)}, u32[]{:S(2)}) async-start(bf16[4,2,6144]{2,1,0:T(2,128)(2,1)} %reshape.273), calls=%async_computation.5 | async-start | bytes 196608 | tf_op jit(solution)/shard_map/all_to_all | solution.py:270
  179.6 1.6 convert_element_type.213
  181.9 1.7 reshape.274
  183.6 1.5 reduce.5
  190.2 1.5 fusion.17
  192.6 8.3 %reduce-scatter.9.cloned.1.call-done = bf16[384,64]{1,0:T(8,128)(2,1)} async-done(((bf16[768,64]{1,0:T(8,128)(2,1)}), bf16[384,64]{1,0:T(8,128)(2,1)}) %reduce-scatter.9.cloned.1.call-update) | async-done | bytes 49168
  202.9 2.5 %psum.14 = f32[64]{0:T(128)S(1)} all-reduce(f32[64]{0:T(128)S(1)} %fusion.106), channel_id=1, replica_groups=mesh['group'=2,'seq'=4,'batch'=2,'mp'=2] {'mp'}, use_global_device_ids=true, to_apply=%region_9.0 | all-reduce | flops 64 | bytes 512 | tf_op jit(solution)/shard_map/psum | solution.py:303
  206.8 1.3 collective-permute-start.2
  208.4 4.5 %collective-permute-start.3 = (bf16[2,384]{1,0:T(2,128)(2,1)S(1)}, bf16[2,384]{1,0:T(2,128)(2,1)S(1)}, u32[]{:S(2)}, u32[]{:S(2)}) collective-permute-start(bf16[2,384]{1,0:T(2,128)(2,1)S(1)} %get-tuple-element.93), channel_id=1, source_target_pairs={{0,4},{4,8},{8,12},{1,5},{5,9},{9,13},{2,6},{6,10},{10,14},{3,7},{... | collective-permute-start | bytes 4616 | tf_op jit(solution)/shard_map/ppermute | solution.py:21
  216.2 19.2 %all-reduce.2.cloned.1.call-done = bf16[128,384]{1,0:T(8,128)(2,1)} async-done(((bf16[128,384]{1,0:T(8,128)(2,1)}), bf16[128,384]{1,0:T(8,128)(2,1)}) %all-reduce.2.cloned.1.call-update) | async-done | bytes 98320 | tf_op jit(solution)/shard_map/psum | solution.py:324
  236.5 1.7 fusion.60
  (154 shorter events, 43.7 us)
Async XLA Ops:
  7.2 13.7 %copy-start.4 = (bf16[1,128,384]{2,1,0:T(8,128)(2,1)S(1)}, bf16[1,128,384]{2,1,0:T(8,128)(2,1)}, u32[]{:S(2)}) copy-start(bf16[1,128,384]{2,1,0:T(8,128)(2,1)} %param.7) | copy-start | bytes 294916
  7.2 40.5 %all-gather.4.cloned.1.call-start = ((), (), s32[]{:S(2)}) async-start(), calls=%async_computation.8 | async-start | bytes 1843200 | tf_op jit(solution)/shard_map/all_gather | solution.py:112
  7.9 80.5 %all-gather.6.cloned.1.call-start = ((), (), s32[]{:S(2)}) async-start(), calls=%async_computation.9 | async-start | bytes 2211840 | tf_op jit(solution)/shard_map/all_gather | solution.py:133
  10.4 6.3 %collective-permute-start = (bf16[2,2,384]{2,1,0:T(2,128)(2,1)S(1)}, bf16[2,2,384]{2,1,0:T(2,128)(2,1)S(1)}, u32[]{:S(2)}, u32[]{:S(2)}) collective-permute-start(bf16[2,2,384]{2,1,0:T(2,128)(2,1)S(1)} %get-tuple-element.88), channel_id=1, source_target_pairs={{0,4},{4,8},{8,12},{1,5},{5,9},{9,13},{2,6},{6,10},{10,14},{3,7},{... | collective-permute-start | bytes 9224 | tf_op jit(solution)/shard_map/ppermute | solution.py:21
  15.4 5.5 %collective-permute-start.1 = (bf16[2,2,384]{2,1,0:T(2,128)(2,1)S(1)}, bf16[2,2,384]{2,1,0:T(2,128)(2,1)S(1)}, u32[]{:S(2)}, u32[]{:S(2)}) collective-permute-start(bf16[2,2,384]{2,1,0:T(2,128)(2,1)S(1)} %get-tuple-element.89), channel_id=1, source_target_pairs={{4,0},{8,4},{12,8},{5,1},{9,5},{13,9},{6,2},{10,6},{14,10},{7,3},{... | collective-permute-start | bytes 9224 | tf_op jit(solution)/shard_map/ppermute | solution.py:23
  47.6 2.6 %copy-start.1 = (bf16[5,384,384]{2,1,0:T(8,128)(2,1)S(1)}, bf16[5,384,384]{2,1,0:T(8,128)(2,1)}, u32[]{:S(2)}) copy-start(bf16[5,384,384]{2,1,0:T(8,128)(2,1)} %all-gather.4.cloned.1.call-done) | copy-start | bytes 4423684
  50.2 0.7 copy-start.10
  51.3 84.9 %copy-start.2 = (f32[2,128,384]{2,1,0:T(8,128)}, f32[2,128,384]{2,1,0:T(8,128)S(1)}, u32[]{:S(2)}) copy-start(f32[2,128,384]{2,1,0:T(8,128)S(1)} %get-tuple-element.95) | copy-start | bytes 1179652
  51.3 37.1 %copy-start.9 = (f32[768]{0:T(1024)S(1)}, f32[768]{0:T(1024)}, u32[]{:S(2)}) copy-start(f32[768]{0:T(1024)} %param.11) | copy-start | bytes 9220
  91.5 9.1 %all-to-all-start = ((bf16[4,2,6144]{2,1,0:T(2,128)(2,1)}), bf16[4,2,6144]{2,1,0:T(2,128)(2,1)S(1)}, u32[]{:S(2)}, u32[]{:S(2)}) async-start(bf16[4,2,6144]{2,1,0:T(2,128)(2,1)} %reshape.242), calls=%async_computation | async-start | bytes 196608 | tf_op jit(solution)/shard_map/all_to_all | solution.py:161
  100.6 9.6 %all-to-all-start.1 = ((bf16[4,2,12288]{2,1,0:T(2,128)(2,1)}), bf16[4,2,12288]{2,1,0:T(2,128)(2,1)S(1)}, u32[]{:S(2)}, u32[]{:S(2)}) async-start(bf16[4,2,12288]{2,1,0:T(2,128)(2,1)} %reshape_reshape.4), calls=%async_computation.1 | async-start | bytes 393216 | tf_op jit(solution)/shard_map/all_to_all | solution.py:162
  110.6 6.0 %copy-start.8 = (bf16[384,192]{0,1:T(8,128)(2,1)S(1)}, bf16[384,192]{0,1:T(8,128)(2,1)}, u32[]{:S(2)}) copy-start(bf16[384,192]{0,1:T(8,128)(2,1)} %param.13) | copy-start | bytes 442372
  113.2 20.2 %all-to-all-start.2 = ((bf16[4,2,6144]{2,1,0:T(2,128)(2,1)}), bf16[4,2,6144]{2,1,0:T(2,128)(2,1)S(1)}, u32[]{:S(2)}, u32[]{:S(2)}) async-start(bf16[4,2,6144]{2,1,0:T(2,128)(2,1)} %copy.103), calls=%async_computation.2 | async-start | bytes 196608 | tf_op jit(solution)/shard_map/all_to_all | solution.py:179
  116.6 26.5 %reduce-scatter.7.cloned.1.call-start = ((), (), s32[]{:S(2)}) async-start(), calls=%async_computation.11 | async-start | bytes 294912
  148.7 10.5 %all-to-all-start.3 = ((bf16[4,2,3072]{2,1,0:T(2,128)(2,1)}), bf16[4,2,3072]{2,1,0:T(2,128)(2,1)S(1)}, u32[]{:S(2)}, u32[]{:S(2)}) async-start(bf16[4,2,3072]{2,1,0:T(2,128)(2,1)} %reshape.271), calls=%async_computation.3 | async-start | bytes 98304 | tf_op jit(solution)/shard_map/all_to_all | solution.py:252
  162.6 8.9 %all-to-all-start.4 = ((bf16[4,2,3072]{2,1,0:T(2,128)(2,1)}), bf16[4,2,3072]{2,1,0:T(2,128)(2,1)S(1)}, u32[]{:S(2)}, u32[]{:S(2)}) async-start(bf16[4,2,3072]{2,1,0:T(2,128)(2,1)} %reshape.275), calls=%async_computation.4 | async-start | bytes 98304 | tf_op jit(solution)/shard_map/all_to_all | solution.py:263
  171.5 0.6 copy-start.7
  172.1 9.8 %all-to-all-start.5 = ((bf16[4,2,6144]{2,1,0:T(2,128)(2,1)}), bf16[4,2,6144]{2,1,0:T(2,128)(2,1)}, u32[]{:S(2)}, u32[]{:S(2)}) async-start(bf16[4,2,6144]{2,1,0:T(2,128)(2,1)} %reshape.273), calls=%async_computation.5 | async-start | bytes 196608 | tf_op jit(solution)/shard_map/all_to_all | solution.py:270
  176.0 14.2 %copy-start = (bf16[3,768,384]{2,1,0:T(8,128)(2,1)S(1)}, bf16[3,768,384]{2,1,0:T(8,128)(2,1)}, u32[]{:S(2)}) copy-start(bf16[3,768,384]{2,1,0:T(8,128)(2,1)} %all-gather.6.cloned.1.call-done) | copy-start | bytes 5308420
  176.1 24.8 %reduce-scatter.9.cloned.1.call-start = ((), (), s32[]{:S(2)}) async-start(), calls=%async_computation.12 | async-start | bytes 294912
  191.7 14.9 %copy-start.3 = (f32[2,128,384]{2,1,0:T(8,128)S(1)}, f32[2,128,384]{2,1,0:T(8,128)}, u32[]{:S(2)}) copy-start(f32[2,128,384]{2,1,0:T(8,128)} %copy-done.2) | copy-start | bytes 1179652
  191.7 16.4 %copy-start.6 = (f32[64,2,384]{2,1,0:T(2,128)S(1)}, f32[64,2,384]{2,1,0:T(2,128)}, u32[]{:S(2)}) copy-start(f32[64,2,384]{2,1,0:T(2,128)} %squeeze.90) | copy-start | bytes 589828
  192.6 42.9 %all-reduce.2.cloned.1.call-start = ((), (), s32[]{:S(2)}) async-start(), calls=%async_computation.10 | async-start | bytes 196608 | tf_op jit(solution)/shard_map/psum | solution.py:324
  206.8 6.4 %collective-permute-start.2 = (bf16[2,384]{1,0:T(2,128)(2,1)S(1)}, bf16[2,384]{1,0:T(2,128)(2,1)S(1)}, u32[]{:S(2)}, u32[]{:S(2)}) collective-permute-start(bf16[2,384]{1,0:T(2,128)(2,1)S(1)} %get-tuple-element.92), channel_id=1, source_target_pairs={{4,0},{8,4},{12,8},{5,1},{9,5},{13,9},{6,2},{10,6},{14,10},{7,3},{... | collective-permute-start | bytes 4616 | tf_op jit(solution)/shard_map/ppermute | solution.py:23
  208.4 5.8 %collective-permute-start.3 = (bf16[2,384]{1,0:T(2,128)(2,1)S(1)}, bf16[2,384]{1,0:T(2,128)(2,1)S(1)}, u32[]{:S(2)}, u32[]{:S(2)}) collective-permute-start(bf16[2,384]{1,0:T(2,128)(2,1)S(1)} %get-tuple-element.93), channel_id=1, source_target_pairs={{0,4},{4,8},{8,12},{1,5},{5,9},{9,13},{2,6},{6,10},{10,14},{3,7},{... | collective-permute-start | bytes 4616 | tf_op jit(solution)/shard_map/ppermute | solution.py:21
  213.4 23.1 %copy-start.5 = (f32[1,128,384]{2,1,0:T(8,128)S(1)}, f32[1,128,384]{2,1,0:T(8,128)}, u32[]{:S(2)}) copy-start(f32[1,128,384]{2,1,0:T(8,128)} %param.8) | copy-start | bytes 589828
Sparse Core Ops, SparseCore 0:
  9.6 38.0 all-gather.3
  49.2 39.1 all-gather.5
  135.6 7.4 reduce-scatter.6
  192.7 8.1 reduce-scatter.8
  215.7 19.7 all-reduce.1
where the time goes:
time: 246 us; the launch traced here: 245 us
  waiting for transfers between devices  120 us (49%)
  starting transfers between devices  34.4 us (14%)
  local copies, waits for them, and re-layouts  27.7 us (11%)
  blocking collectives  23.1 us (9%)
  between operations  14.6 us (6%)
  other arithmetic  13.9 us (6%)
  matrix products  11.3 us (5%)
    all_gather x1, waiting for transfers between devices, forward(): lax.all_gather(qkv_weight, 'seq', axis=1, tiled=True)  34.5 us
    all_gather x1, waiting for transfers between devices, forward(): piece = lax.all_gather(conv_weight, 'seq', axis=1, tiled=True)  26.7 us
    psum x1, waiting for transfers between devices, shards(): lax.psum(running.astype(jnp.bfloat16), 'mp').astype(jnp.float32)  19.2 us
    all_gather x1, blocking collectives, forward(): lax.all_gather(out_weight, 'seq', axis=1, tiled=True)  16.8 us
    unnamed x7, waiting for transfers between devices  14.9 us
    unnamed x34, local copies, waits for them, and re-layouts  9.74 us
    ppermute x2, starting transfers between devices, with_halo(): lax.ppermute(tail, axis, [(i, (i + 1) % count) for i in range(ends)])  9.49 us
    all_to_all x1, waiting for transfers between devices, forward(): lax.all_to_all(keyval_send, 'seq', split_axis=0, concat_axis=2, tiled=True)  5.54 us
  transfers between devices with their start and end apart: 15, of which 12 were waited for; matrix products, arithmetic and copies ran while one was open for 8% of the time, Pallas kernels for 0%

commit v1 on v0

--- a/solution.py
+++ b/solution.py
@@ -321,7 +321,11 @@
             piece[offset],
             preferred_element_type=jnp.float32,
         )
-    input_grad = lax.psum(running.astype(jnp.bfloat16), "mp").astype(jnp.float32)
+
+    def prepare_rails(piece_in):
+        return jnp.sum(lax.all_gather(piece_in, "mp"), 0)
+
+    input_grad = prepare_rails(running.astype(jnp.bfloat16)).astype(jnp.float32)
     new_noise = noise[0] + step_size * input_grad * lax.rsqrt(
         jnp.mean(input_grad * input_grad, axis=1, keepdims=True) + epsilon
     )

time: 246 us -> 226 us (0.919)
  waiting for transfers between devices: 120 us -> 99.9 us
    psum x1 -> x0, waiting for transfers between devices: 19.2 us -> none  [shards(): lax.psum(running.astype(jnp.bfloat16), 'mp').astype(jnp.float32)]
    unnamed x7 -> x6, waiting for transfers between devices: 14.9 us -> 14.3 us
  transfers between devices with their start and end apart: 15 -> 14, of which waited for: 12 -> 11; matrix products, arithmetic and copies ran while one was open for 8% -> 9% of each run, Pallas kernels for 0% -> 0%
where the time goes in v1:
time: 226 us; the launch traced here: 224 us
  waiting for transfers between devices  99.9 us (44%)
  starting transfers between devices  34.4 us (15%)
  local copies, waits for them, and re-layouts  27.7 us (12%)
  blocking collectives  25 us (11%)
  between operations  14.6 us (6%)
  other arithmetic  12.1 us (5%)
  matrix products  10.7 us (5%)
    all_gather x1, waiting for transfers between devices, forward(): lax.all_gather(qkv_weight, 'seq', axis=1, tiled=True)  34.5 us
    all_gather x1, waiting for transfers between devices, forward(): piece = lax.all_gather(conv_weight, 'seq', axis=1, tiled=True)  26.7 us
    all_gather x1, blocking collectives, forward(): lax.all_gather(out_weight, 'seq', axis=1, tiled=True)  16.8 us
    unnamed x6, waiting for transfers between devices  14.3 us
    unnamed x34, local copies, waits for them, and re-layouts  9.74 us
    ppermute x2, starting transfers between devices, with_halo(): lax.ppermute(tail, axis, [(i, (i + 1) % count) for i in range(ends)])  9.49 us
    all_to_all x1, waiting for transfers between devices, forward(): lax.all_to_all(keyval_send, 'seq', split_axis=0, concat_axis=2, tiled=True)  5.54 us
    all_to_all x1, waiting for transfers between devices, shards(): lax.all_to_all(grad_send, 'seq', split_axis=0, concat_axis=1, tiled=True)  5.5 us
  transfers between devices with their start and end apart: 14, of which 11 were waited for; matrix products, arithmetic and copies ran while one was open for 9% of the time, Pallas kernels for 0%

profile of v1, /device:TPU:0, one launch (start us, length us, event | category | flops | bytes accessed | tf_op | source)
XLA Modules:
  0.0 224.3 jit_solution(7525956830794454648)
XLA Ops:
  10.4 4.9 %collective-permute-start = (bf16[2,2,384]{2,1,0:T(2,128)(2,1)S(1)}, bf16[2,2,384]{2,1,0:T(2,128)(2,1)S(1)}, u32[]{:S(2)}, u32[]{:S(2)}) collective-permute-start(bf16[2,2,384]{2,1,0:T(2,128)(2,1)S(1)} %get-tuple-element.88), channel_id=1, source_target_pairs={{0,4},{4,8},{8,12},{1,5},{5,9},{9,13},{2,6},{6,10},{10,14},{3,7},{... | collective-permute-start | bytes 9224 | tf_op jit(solution)/shard_map/ppermute | solution.py:21
  15.4 1.3 collective-permute-start.1
  16.7 4.2 %collective-permute-done.1 = bf16[2,2,384]{2,1,0:T(2,128)(2,1)S(1)} collective-permute-done((bf16[2,2,384]{2,1,0:T(2,128)(2,1)S(1)}, bf16[2,2,384]{2,1,0:T(2,128)(2,1)S(1)}, u32[]{:S(2)}, u32[]{:S(2)}) %collective-permute-start.1) | collective-permute-done | bytes 3104 | tf_op jit(solution)/shard_map/ppermute | solution.py:23
  20.9 26.7 %all-gather.5.cloned.1.call-done = bf16[5,384,384]{2,1,0:T(8,128)(2,1)} async-done(((bf16[5,96,384]{2,1,0:T(8,128)(2,1)}), bf16[5,384,384]{2,1,0:T(8,128)(2,1)}) %all-gather.5.cloned.1.call-update) | async-done | bytes 1474576 | tf_op jit(solution)/shard_map/all_gather | solution.py:112
  47.6 1.3 fusion.38
  49.0 1.2 fusion.42
  51.9 1.9 all-gather
  54.0 34.5 %all-gather.7.cloned.1.call-done = bf16[3,768,384]{2,1,0:T(8,128)(2,1)} async-done(((bf16[3,192,384]{2,1,0:T(8,128)(2,1)}), bf16[3,768,384]{2,1,0:T(8,128)(2,1)}) %all-gather.7.cloned.1.call-update) | async-done | bytes 1769488 | tf_op jit(solution)/shard_map/all_gather | solution.py:133
  88.5 2.0 fusion.8
  91.5 3.3 %all-to-all-start = ((bf16[4,2,6144]{2,1,0:T(2,128)(2,1)}), bf16[4,2,6144]{2,1,0:T(2,128)(2,1)S(1)}, u32[]{:S(2)}, u32[]{:S(2)}) async-start(bf16[4,2,6144]{2,1,0:T(2,128)(2,1)} %reshape.270), calls=%async_computation | async-start | bytes 196608 | tf_op jit(solution)/shard_map/all_to_all | solution.py:161
  96.3 4.3 %all-to-all-done = bf16[4,2,6144]{2,1,0:T(2,128)(2,1)S(1)} async-done(((bf16[4,2,6144]{2,1,0:T(2,128)(2,1)}), bf16[4,2,6144]{2,1,0:T(2,128)(2,1)S(1)}, u32[]{:S(2)}, u32[]{:S(2)}) %all-to-all-start) | async-done | bytes 98336 | tf_op jit(solution)/shard_map/all_to_all | solution.py:161
  100.6 3.4 %all-to-all-start.1 = ((bf16[4,2,12288]{2,1,0:T(2,128)(2,1)}), bf16[4,2,12288]{2,1,0:T(2,128)(2,1)S(1)}, u32[]{:S(2)}, u32[]{:S(2)}) async-start(bf16[4,2,12288]{2,1,0:T(2,128)(2,1)} %reshape_reshape.4), calls=%async_computation.1 | async-start | bytes 393216 | tf_op jit(solution)/shard_map/all_to_all | solution.py:162
  104.6 5.5 %all-to-all-done.1 = bf16[4,2,12288]{2,1,0:T(2,128)(2,1)S(1)} async-done(((bf16[4,2,12288]{2,1,0:T(2,128)(2,1)}), bf16[4,2,12288]{2,1,0:T(2,128)(2,1)S(1)}, u32[]{:S(2)}, u32[]{:S(2)}) %all-to-all-start.1) | async-done | bytes 196640 | tf_op jit(solution)/shard_map/all_to_all | solution.py:162
  113.2 3.3 %all-to-all-start.2 = ((bf16[4,2,6144]{2,1,0:T(2,128)(2,1)}), bf16[4,2,6144]{2,1,0:T(2,128)(2,1)S(1)}, u32[]{:S(2)}, u32[]{:S(2)}) async-start(bf16[4,2,6144]{2,1,0:T(2,128)(2,1)} %copy.103), calls=%async_computation.2 | async-start | bytes 196608 | tf_op jit(solution)/shard_map/all_to_all | solution.py:179
  116.6 16.8 %all_gather.27 = bf16[384,768]{0,1:T(8,128)(2,1)S(1)} all-gather(bf16[384,192]{0,1:T(8,128)(2,1)S(1)} %copy-done.8), channel_id=1, replica_groups=mesh['group'=2,'seq'=4,'batch'=2,'mp'=2] {'seq'}, dimensions={1}, use_global_device_ids=true | all-gather | bytes 737280 | tf_op jit(solution)/shard_map/all_gather | solution.py:188
  137.8 5.3 %reduce-scatter.7.cloned.1.call-done = bf16[384,128]{1,0:T(8,128)(2,1)} async-done(((bf16[768,128]{1,0:T(8,128)(2,1)}), bf16[384,128]{1,0:T(8,128)(2,1)}) %reduce-scatter.7.cloned.1.call-update) | async-done | bytes 98320
  144.3 1.9 all_gather.28
  148.7 4.8 %all-to-all-start.3 = ((bf16[4,2,3072]{2,1,0:T(2,128)(2,1)}), bf16[4,2,3072]{2,1,0:T(2,128)(2,1)S(1)}, u32[]{:S(2)}, u32[]{:S(2)}) async-start(bf16[4,2,3072]{2,1,0:T(2,128)(2,1)} %reshape.301), calls=%async_computation.3 | async-start | bytes 98304 | tf_op jit(solution)/shard_map/all_to_all | solution.py:252
  153.7 5.5 %all-to-all-done.3 = bf16[4,2,3072]{2,1,0:T(2,128)(2,1)S(1)} async-done(((bf16[4,2,3072]{2,1,0:T(2,128)(2,1)}), bf16[4,2,3072]{2,1,0:T(2,128)(2,1)S(1)}, u32[]{:S(2)}, u32[]{:S(2)}) %all-to-all-start.3) | async-done | bytes 49184 | tf_op jit(solution)/shard_map/all_to_all | solution.py:252
  162.6 3.5 %all-to-all-start.4 = ((bf16[4,2,3072]{2,1,0:T(2,128)(2,1)}), bf16[4,2,3072]{2,1,0:T(2,128)(2,1)S(1)}, u32[]{:S(2)}, u32[]{:S(2)}) async-start(bf16[4,2,3072]{2,1,0:T(2,128)(2,1)} %reshape.305), calls=%async_computation.4 | async-start | bytes 98304 | tf_op jit(solution)/shard_map/all_to_all | solution.py:263
  166.3 1.2 reduce.11
  168.3 3.2 %all-to-all-done.4 = bf16[4,2,3072]{2,1,0:T(2,128)(2,1)S(1)} async-done(((bf16[4,2,3072]{2,1,0:T(2,128)(2,1)}), bf16[4,2,3072]{2,1,0:T(2,128)(2,1)S(1)}, u32[]{:S(2)}, u32[]{:S(2)}) %all-to-all-start.4) | async-done | bytes 49184 | tf_op jit(solution)/shard_map/all_to_all | solution.py:263
  172.1 3.9 %all-to-all-start.5 = ((bf16[4,2,6144]{2,1,0:T(2,128)(2,1)}), bf16[4,2,6144]{2,1,0:T(2,128)(2,1)}, u32[]{:S(2)}, u32[]{:S(2)}) async-start(bf16[4,2,6144]{2,1,0:T(2,128)(2,1)} %reshape.303), calls=%async_computation.5 | async-start | bytes 196608 | tf_op jit(solution)/shard_map/all_to_all | solution.py:270
  179.6 1.6 convert_element_type.227
  181.9 1.7 reshape.304
  183.6 1.5 reduce.6
  190.2 1.5 fusion.17
  193.2 7.7 %reduce-scatter.9.cloned.1.call-done = bf16[384,64]{1,0:T(8,128)(2,1)} async-done(((bf16[768,64]{1,0:T(8,128)(2,1)}), bf16[384,64]{1,0:T(8,128)(2,1)}) %reduce-scatter.9.cloned.1.call-update) | async-done | bytes 49168
  202.9 2.5 %psum.7 = f32[64]{0:T(128)S(1)} all-reduce(f32[64]{0:T(128)S(1)} %fusion.106), channel_id=1, replica_groups=mesh['group'=2,'seq'=4,'batch'=2,'mp'=2] {'mp'}, use_global_device_ids=true, to_apply=%region_9.0 | all-reduce | flops 64 | bytes 512 | tf_op jit(solution)/shard_map/psum | solution.py:303
  206.8 1.3 collective-permute-start.2
  208.4 4.5 %collective-permute-start.3 = (bf16[2,384]{1,0:T(2,128)(2,1)S(1)}, bf16[2,384]{1,0:T(2,128)(2,1)S(1)}, u32[]{:S(2)}, u32[]{:S(2)}) collective-permute-start(bf16[2,384]{1,0:T(2,128)(2,1)S(1)} %get-tuple-element.93), channel_id=1, source_target_pairs={{0,4},{4,8},{8,12},{1,5},{5,9},{9,13},{2,6},{6,10},{10,14},{3,7},{... | collective-permute-start | bytes 4616 | tf_op jit(solution)/shard_map/ppermute | solution.py:21
  214.9 1.9 all-gather.1
  (153 shorter events, 41.6 us)
Async XLA Ops:
  7.2 13.7 %copy-start.4 = (bf16[1,128,384]{2,1,0:T(8,128)(2,1)S(1)}, bf16[1,128,384]{2,1,0:T(8,128)(2,1)}, u32[]{:S(2)}) copy-start(bf16[1,128,384]{2,1,0:T(8,128)(2,1)} %param.7) | copy-start | bytes 294916
  7.2 40.5 %all-gather.5.cloned.1.call-start = ((), (), s32[]{:S(2)}) async-start(), calls=%async_computation.8 | async-start | bytes 1843200 | tf_op jit(solution)/shard_map/all_gather | solution.py:112
  7.9 80.5 %all-gather.7.cloned.1.call-start = ((), (), s32[]{:S(2)}) async-start(), calls=%async_computation.9 | async-start | bytes 2211840 | tf_op jit(solution)/shard_map/all_gather | solution.py:133
  10.4 6.3 %collective-permute-start = (bf16[2,2,384]{2,1,0:T(2,128)(2,1)S(1)}, bf16[2,2,384]{2,1,0:T(2,128)(2,1)S(1)}, u32[]{:S(2)}, u32[]{:S(2)}) collective-permute-start(bf16[2,2,384]{2,1,0:T(2,128)(2,1)S(1)} %get-tuple-element.88), channel_id=1, source_target_pairs={{0,4},{4,8},{8,12},{1,5},{5,9},{9,13},{2,6},{6,10},{10,14},{3,7},{... | collective-permute-start | bytes 9224 | tf_op jit(solution)/shard_map/ppermute | solution.py:21
  15.4 5.5 %collective-permute-start.1 = (bf16[2,2,384]{2,1,0:T(2,128)(2,1)S(1)}, bf16[2,2,384]{2,1,0:T(2,128)(2,1)S(1)}, u32[]{:S(2)}, u32[]{:S(2)}) collective-permute-start(bf16[2,2,384]{2,1,0:T(2,128)(2,1)S(1)} %get-tuple-element.89), channel_id=1, source_target_pairs={{4,0},{8,4},{12,8},{5,1},{9,5},{13,9},{6,2},{10,6},{14,10},{7,3},{... | collective-permute-start | bytes 9224 | tf_op jit(solution)/shard_map/ppermute | solution.py:23
  47.6 2.6 %copy-start.1 = (bf16[5,384,384]{2,1,0:T(8,128)(2,1)S(1)}, bf16[5,384,384]{2,1,0:T(8,128)(2,1)}, u32[]{:S(2)}) copy-start(bf16[5,384,384]{2,1,0:T(8,128)(2,1)} %all-gather.5.cloned.1.call-done) | copy-start | bytes 4423684
  50.2 0.7 copy-start.10
  51.3 84.9 %copy-start.2 = (f32[2,128,384]{2,1,0:T(8,128)}, f32[2,128,384]{2,1,0:T(8,128)S(1)}, u32[]{:S(2)}) copy-start(f32[2,128,384]{2,1,0:T(8,128)S(1)} %get-tuple-element.95) | copy-start | bytes 1179652
  51.3 37.1 %copy-start.9 = (f32[768]{0:T(1024)S(1)}, f32[768]{0:T(1024)}, u32[]{:S(2)}) copy-start(f32[768]{0:T(1024)} %param.11) | copy-start | bytes 9220
  91.5 9.1 %all-to-all-start = ((bf16[4,2,6144]{2,1,0:T(2,128)(2,1)}), bf16[4,2,6144]{2,1,0:T(2,128)(2,1)S(1)}, u32[]{:S(2)}, u32[]{:S(2)}) async-start(bf16[4,2,6144]{2,1,0:T(2,128)(2,1)} %reshape.270), calls=%async_computation | async-start | bytes 196608 | tf_op jit(solution)/shard_map/all_to_all | solution.py:161
  100.6 9.6 %all-to-all-start.1 = ((bf16[4,2,12288]{2,1,0:T(2,128)(2,1)}), bf16[4,2,12288]{2,1,0:T(2,128)(2,1)S(1)}, u32[]{:S(2)}, u32[]{:S(2)}) async-start(bf16[4,2,12288]{2,1,0:T(2,128)(2,1)} %reshape_reshape.4), calls=%async_computation.1 | async-start | bytes 393216 | tf_op jit(solution)/shard_map/all_to_all | solution.py:162
  110.6 6.0 %copy-start.8 = (bf16[384,192]{0,1:T(8,128)(2,1)S(1)}, bf16[384,192]{0,1:T(8,128)(2,1)}, u32[]{:S(2)}) copy-start(bf16[384,192]{0,1:T(8,128)(2,1)} %param.13) | copy-start | bytes 442372
  113.2 20.2 %all-to-all-start.2 = ((bf16[4,2,6144]{2,1,0:T(2,128)(2,1)}), bf16[4,2,6144]{2,1,0:T(2,128)(2,1)S(1)}, u32[]{:S(2)}, u32[]{:S(2)}) async-start(bf16[4,2,6144]{2,1,0:T(2,128)(2,1)} %copy.103), calls=%async_computation.2 | async-start | bytes 196608 | tf_op jit(solution)/shard_map/all_to_all | solution.py:179
  116.6 26.5 %reduce-scatter.7.cloned.1.call-start = ((), (), s32[]{:S(2)}) async-start(), calls=%async_computation.10 | async-start | bytes 294912
  148.7 10.5 %all-to-all-start.3 = ((bf16[4,2,3072]{2,1,0:T(2,128)(2,1)}), bf16[4,2,3072]{2,1,0:T(2,128)(2,1)S(1)}, u32[]{:S(2)}, u32[]{:S(2)}) async-start(bf16[4,2,3072]{2,1,0:T(2,128)(2,1)} %reshape.301), calls=%async_computation.3 | async-start | bytes 98304 | tf_op jit(solution)/shard_map/all_to_all | solution.py:252
  162.6 8.9 %all-to-all-start.4 = ((bf16[4,2,3072]{2,1,0:T(2,128)(2,1)}), bf16[4,2,3072]{2,1,0:T(2,128)(2,1)S(1)}, u32[]{:S(2)}, u32[]{:S(2)}) async-start(bf16[4,2,3072]{2,1,0:T(2,128)(2,1)} %reshape.305), calls=%async_computation.4 | async-start | bytes 98304 | tf_op jit(solution)/shard_map/all_to_all | solution.py:263
  171.5 0.6 copy-start.7
  172.1 9.8 %all-to-all-start.5 = ((bf16[4,2,6144]{2,1,0:T(2,128)(2,1)}), bf16[4,2,6144]{2,1,0:T(2,128)(2,1)}, u32[]{:S(2)}, u32[]{:S(2)}) async-start(bf16[4,2,6144]{2,1,0:T(2,128)(2,1)} %reshape.303), calls=%async_computation.5 | async-start | bytes 196608 | tf_op jit(solution)/shard_map/all_to_all | solution.py:270
  176.0 14.2 %copy-start = (bf16[3,768,384]{2,1,0:T(8,128)(2,1)S(1)}, bf16[3,768,384]{2,1,0:T(8,128)(2,1)}, u32[]{:S(2)}) copy-start(bf16[3,768,384]{2,1,0:T(8,128)(2,1)} %all-gather.7.cloned.1.call-done) | copy-start | bytes 5308420
  176.1 24.8 %reduce-scatter.9.cloned.1.call-start = ((), (), s32[]{:S(2)}) async-start(), calls=%async_computation.11 | async-start | bytes 294912
  191.7 14.9 %copy-start.3 = (f32[2,128,384]{2,1,0:T(8,128)S(1)}, f32[2,128,384]{2,1,0:T(8,128)}, u32[]{:S(2)}) copy-start(f32[2,128,384]{2,1,0:T(8,128)} %copy-done.2) | copy-start | bytes 1179652
  191.7 16.4 %copy-start.6 = (f32[64,2,384]{2,1,0:T(2,128)S(1)}, f32[64,2,384]{2,1,0:T(2,128)}, u32[]{:S(2)}) copy-start(f32[64,2,384]{2,1,0:T(2,128)} %squeeze.87) | copy-start | bytes 589828
  206.8 6.4 %collective-permute-start.2 = (bf16[2,384]{1,0:T(2,128)(2,1)S(1)}, bf16[2,384]{1,0:T(2,128)(2,1)S(1)}, u32[]{:S(2)}, u32[]{:S(2)}) collective-permute-start(bf16[2,384]{1,0:T(2,128)(2,1)S(1)} %get-tuple-element.92), channel_id=1, source_target_pairs={{4,0},{8,4},{12,8},{5,1},{9,5},{13,9},{6,2},{10,6},{14,10},{7,3},{... | collective-permute-start | bytes 4616 | tf_op jit(solution)/shard_map/ppermute | solution.py:23
  208.4 5.8 %collective-permute-start.3 = (bf16[2,384]{1,0:T(2,128)(2,1)S(1)}, bf16[2,384]{1,0:T(2,128)(2,1)S(1)}, u32[]{:S(2)}, u32[]{:S(2)}) collective-permute-start(bf16[2,384]{1,0:T(2,128)(2,1)S(1)} %get-tuple-element.93), channel_id=1, source_target_pairs={{0,4},{4,8},{8,12},{1,5},{5,9},{9,13},{2,6},{6,10},{10,14},{3,7},{... | collective-permute-start | bytes 4616 | tf_op jit(solution)/shard_map/ppermute | solution.py:21
  213.4 3.6 %copy-start.5 = (f32[1,128,384]{2,1,0:T(8,128)S(1)}, f32[1,128,384]{2,1,0:T(8,128)}, u32[]{:S(2)}) copy-start(f32[1,128,384]{2,1,0:T(8,128)} %param.8) | copy-start | bytes 589828
Sparse Core Ops, SparseCore 0:
  9.6 38.0 all-gather.4
  49.2 39.1 all-gather.6
  135.6 7.4 reduce-scatter.6
  192.7 8.1 reduce-scatter.8
